TPU v7x, 32 devices: a whole 2x2x4 slice. The times are simulated.
32 devices in a mesh: ctx: 8 (over z, y), dp: 2 (over x), section: 2 (over core).
Axes of the slice: x: 2, y: 2, z: 4, core: 2. Of those that a mesh axis runs over, the one named last changes fastest.
Arguments:
- normed: bfloat16 [2, 3072, 1024], P('dp', 'ctx'), may hold values from -40 to 40
- w_query: bfloat16 [1024, 1024], P('dp', 'section'), may hold values from -0.1875 to 0.1875
- w_key: bfloat16 [1024, 1024], P('dp', 'section'), may hold values from -0.28125 to 0.28125
- w_value: bfloat16 [1024, 1024], P('dp', 'section'), may hold values from -0.1875 to 0.1875
- block_mask: int32 [24, 7], replicated, may hold values from 0 to 1, as said below
- cotangent: bfloat16 [2, 3072, 1024], P('dp', 'ctx', 'section'), may hold values from -8 to 8
Outputs:
- attended: bfloat16 [2, 3072, 1024], P('dp', 'ctx', 'section')
- grad_input: bfloat16 [2, 3072, 1024], P('dp', 'ctx')
- grad_weights: float32 [1024, 3, 1024], P(('ctx', 'dp'), None, 'section')
Inputs may be any that keep to these rules, and one draw needn't show every extreme that they name: `block_mask`: every row has a 1 in column 3; no row names a key block outside 0 to 23; a row holds at most 5 ones, and some row holds exactly 5.
All inputs are finite; a program needn't handle non-finite values.
Results may differ from a plain program's by a relative error of at most 0.014.
The roundings to bfloat16 on the way count: a program that leaves them out, or rounds other values in their place, can miss the bound.
Values may be sent and summed in bfloat16 or wider, within the bound.
No kernel may reach another device: no remote copies, remote signals or barrier semaphores. Data moves between devices by JAX's collectives and lax.ppermute only.
A program may use at most 64 MiB of HBM per device.

v0:
```python
import jax
import jax.numpy as jnp
from jax import lax
from jax.sharding import PartitionSpec as P

HD = 64
BLOCK = 128
REACH = 3


def extended(cells, sides, width):
    for axis, dim in sides:
        count = lax.axis_size(axis)
        ends = count - 1
        head = lax.slice_in_dim(cells, 0, width, axis=dim)
        tail = lax.slice_in_dim(cells, cells.shape[dim] - width, cells.shape[dim], axis=dim)
        cells = jnp.concatenate(
            [
                lax.ppermute(tail, axis, [(i, (i + 1) % count) for i in range(ends)]),
                cells,
                lax.ppermute(head, axis, [((i + 1) % count, i) for i in range(ends)]),
            ],
            axis=dim,
        )
    return cells


def shifted(value, axis, steps):
    count = lax.axis_size(axis)
    leading, last = (max(0, -steps), min(count, count - steps))
    return lax.ppermute(value, axis, [(source, source + steps) for source in range(leading, last)])


def attend(query_block, key_window, seen_slots, score_scale):
    scores = (
        jnp.einsum("qhd,skhd->hqsk", query_block, key_window, preferred_element_type=jnp.float32)
        * score_scale
    )
    is_seen = seen_slots[None, None, :, None] > 0
    row_top = jnp.max(jnp.where(is_seen, scores, -jnp.inf), axis=(2, 3), keepdims=True)
    raised = jnp.where(is_seen, jnp.exp(scores - row_top), 0.0)
    row_total = jnp.sum(raised, axis=(2, 3), keepdims=True)
    return (raised / row_total, row_top, row_total)


def per_device(normed, w_query, w_key, w_value, block_mask, cotangent):
    tokens = normed[0]
    upstream = cotangent[0]
    length = tokens.shape[0]
    features = upstream.shape[1]
    head_count = features // HD
    blocks = length // BLOCK
    frame_len = blocks + 2 * REACH
    span_len = 2 * REACH + 1
    score_scale = HD ** (-0.5)
    query_full, key_full, value_full = (
        lax.all_gather(w_query, "dp", axis=0, tiled=True),
        lax.all_gather(w_key, "dp", axis=0, tiled=True),
        lax.all_gather(w_value, "dp", axis=0, tiled=True),
    )
    queries = jnp.dot(tokens, query_full, preferred_element_type=jnp.float32).astype(jnp.bfloat16)
    key_rows = jnp.dot(tokens, key_full, preferred_element_type=jnp.float32).astype(jnp.bfloat16)
    value_rows = jnp.dot(tokens, value_full, preferred_element_type=jnp.float32).astype(
        jnp.bfloat16
    )
    framed = extended(jnp.stack([key_rows, value_rows]), (("ctx", 1),), REACH * BLOCK)
    framed = framed.reshape(2, frame_len, BLOCK, head_count, HD)
    query_blocks = queries.reshape(blocks, BLOCK, head_count, HD)
    upstream_blocks = upstream.reshape(blocks, BLOCK, head_count, HD)
    first_block = lax.axis_index("ctx") * blocks
    padded_mask = jnp.pad(block_mask, ((REACH, REACH), (0, 0)))
    frame_mask = lax.dynamic_slice(padded_mask, (first_block, 0), (frame_len, span_len))
    own_mask = frame_mask[REACH : REACH + blocks]
    positions = jnp.arange(span_len, dtype=jnp.int32)
    slot_order = jnp.broadcast_to(positions[None, :], (blocks, span_len))
    slot_index = slot_order + jnp.arange(blocks, dtype=jnp.int32)[:, None]

    def windows(block_at):
        picked = lax.dynamic_slice_in_dim(framed, block_at, span_len, 1)
        return (picked[0], picked[1])

    def forward(running, block_at):
        query_block = lax.dynamic_index_in_dim(query_blocks, block_at, 0, False)
        key_window, value_window = windows(block_at)
        seen_slots = lax.dynamic_index_in_dim(own_mask, block_at, 0, False)
        probability, row_top, row_total = attend(query_block, key_window, seen_slots, score_scale)
        mixed_out = jnp.einsum(
            "hqsk,skhd->qhd",
            probability.astype(jnp.bfloat16),
            value_window,
            preferred_element_type=jnp.float32,
        ).astype(jnp.bfloat16)
        return (running, (mixed_out, row_top[:, :, 0, 0], row_total[:, :, 0, 0]))

    block_ids = jnp.arange(blocks, dtype=jnp.int32)
    _, (mixed_outs, row_tops, row_totals) = lax.scan(forward, jnp.zeros((), jnp.float32), block_ids)
    attended = mixed_outs.reshape(1, length, features)

    def backward(running, block_at):
        query_block = lax.dynamic_index_in_dim(query_blocks, block_at, 0, False)
        upstream_block = lax.dynamic_index_in_dim(upstream_blocks, block_at, 0, False)
        key_window, value_window = windows(block_at)
        seen_slots = lax.dynamic_index_in_dim(own_mask, block_at, 0, False)
        probability, _, _ = attend(query_block, key_window, seen_slots, score_scale)
        weights = probability.astype(jnp.bfloat16)
        prob_grad = jnp.einsum(
            "qhd,skhd->hqsk", upstream_block, value_window, preferred_element_type=jnp.float32
        )
        row_delta = jnp.sum(probability * prob_grad, axis=(2, 3), keepdims=True)
        score_grad = (probability * (prob_grad - row_delta)).astype(jnp.bfloat16)
        query_grad = (
            score_scale
            * jnp.einsum(
                "hqsk,skhd->qhd", score_grad, key_window, preferred_element_type=jnp.float32
            )
        ).astype(jnp.bfloat16)
        key_part = score_scale * jnp.einsum(
            "hqsk,qhd->skhd", score_grad, query_block, preferred_element_type=jnp.float32
        )
        value_part = jnp.einsum(
            "hqsk,qhd->skhd", weights, upstream_block, preferred_element_type=jnp.float32
        )
        slot_rows = lax.dynamic_index_in_dim(slot_index, block_at, 0, False)
        running = running.at[0, slot_rows].add(key_part).at[1, slot_rows].add(value_part)
        return (running, (query_grad, row_delta[:, :, 0, 0]))

    start_state = jnp.zeros((2, frame_len, BLOCK, head_count, HD), jnp.float32)
    frame_grads, (query_grads, row_deltas) = lax.scan(backward, start_state, block_ids)
    query_grad = query_grads.reshape(length, features)
    frame_grads = frame_grads.reshape(2, frame_len, BLOCK, features)
    left_side = frame_grads[:, :REACH]
    right_side = frame_grads[:, blocks + REACH :]
    middle = frame_grads[:, REACH : REACH + blocks]
    for offset in (1, -1):
        outgoing = right_side if offset == 1 else left_side
        arrived = shifted(outgoing.astype(jnp.bfloat16), "ctx", offset).astype(outgoing.dtype)
        if offset == 1:
            middle = middle.at[:, :REACH].add(arrived)
        else:
            middle = middle.at[:, blocks - REACH :].add(arrived)
    key_grad = middle[0].reshape(length, features).astype(jnp.bfloat16)
    value_grad = middle[1].reshape(length, features).astype(jnp.bfloat16)
    contract = (((1,), (1,)), ((), ()))
    partial_input = (
        lax.dot_general(query_grad, query_full, contract, preferred_element_type=jnp.float32)
        + lax.dot_general(key_grad, key_full, contract, preferred_element_type=jnp.float32)
        + lax.dot_general(value_grad, value_full, contract, preferred_element_type=jnp.float32)
    )
    grad_input = lax.psum(partial_input.astype(jnp.bfloat16), "section")[None]
    grads_all = jnp.stack([query_grad, key_grad, value_grad], axis=1)
    group_part = lax.psum_scatter(
        jnp.einsum("tr,tcf->rcf", tokens, grads_all, preferred_element_type=jnp.float32).astype(
            jnp.bfloat16
        ),
        "ctx",
        scatter_dimension=0,
        tiled=True,
    )
    summed = lax.psum_scatter(group_part, "dp", scatter_dimension=0, tiled=True).astype(jnp.float32)
    grad_weights = summed / lax.axis_size("dp")
    return (attended, grad_input, grad_weights)


def solution(mesh):
    in_specs = (
        P("dp", "ctx", None),
        P("dp", "section"),
        P("dp", "section"),
        P("dp", "section"),
        P(),
        P("dp", "ctx", "section"),
    )
    out_specs = (P("dp", "ctx", "section"), P("dp", "ctx", None), P(("ctx", "dp"), None, "section"))
    return jax.shard_map(
        per_device, mesh=mesh, in_specs=in_specs, out_specs=out_specs, check_vma=False
    )
```

profile of v0, /device:TPU:0, one launch (start us, length us, event | category | flops | bytes accessed | tf_op | source)
XLA Modules:
  0.0 379.1 jit_solution(11920346828465409349)
XLA Ops:
  9.5 24.1 %all-gather.6.cloned.1.call-done = bf16[1024,512]{1,0:T(8,128)(2,1)} async-done(((bf16[512,512]{1,0:T(8,128)(2,1)}), bf16[1024,512]{1,0:T(8,128)(2,1)}) %all-gather.6.cloned.1.call-update) | async-done | bytes 1048592 | tf_op jit(solution)/shard_map/all_gather | solution.py:59
  33.6 1.8 fusion.44
  35.4 21.1 %all-gather.4.cloned.1.call-done = bf16[1024,512]{1,0:T(8,128)(2,1)} async-done(((bf16[512,512]{1,0:T(8,128)(2,1)}), bf16[1024,512]{1,0:T(8,128)(2,1)}) %all-gather.4.cloned.1.call-update) | async-done | bytes 1048592 | tf_op jit(solution)/shard_map/all_gather | solution.py:58
  56.5 1.8 fusion.43
  60.4 5.5 %collective-permute-start = (bf16[2,384,512]{2,1,0:T(8,128)(2,1)S(1)}, bf16[2,384,512]{2,1,0:T(8,128)(2,1)}, u32[]{:S(2)}, u32[]{:S(2)}) collective-permute-start(bf16[2,384,512]{2,1,0:T(8,128)(2,1)S(1)} %pad_maximum_fusion.1), channel_id=1, source_target_pairs={{0,4},{4,8},{8,12},{12,16},{16,20},{20,24},{24,28},{1,5},{5,9},{9,... | collective-permute-start | bytes 2359304 | tf_op jit(solution)/shard_map/ppermute | solution.py:19
  68.1 11.2 %all-gather.8.cloned.1.call-done = bf16[1024,512]{1,0:T(8,128)(2,1)} async-done(((bf16[512,512]{1,0:T(8,128)(2,1)}), bf16[1024,512]{1,0:T(8,128)(2,1)}) %all-gather.8.cloned.1.call-update) | async-done | bytes 1048592 | tf_op jit(solution)/shard_map/all_gather | solution.py:57
  79.4 1.8 convolution_convert_fusion.1
  82.9 14.1 %collective-permute-done = bf16[2,384,512]{2,1,0:T(8,128)(2,1)} collective-permute-done((bf16[2,384,512]{2,1,0:T(8,128)(2,1)S(1)}, bf16[2,384,512]{2,1,0:T(8,128)(2,1)}, u32[]{:S(2)}, u32[]{:S(2)}) %collective-permute-start) | collective-permute-done | bytes 786464 | tf_op jit(solution)/shard_map/ppermute | solution.py:19
  97.0 1.8 pad_maximum_fusion
  98.8 4.6 %reshape.200 = bf16[2,9,128,8,64]{4,3,2,1,0:T(8,128)(2,1)} reshape(bf16[2,1152,512]{2,1,0:T(8,128)(2,1)S(1)} %pad_maximum_fusion) | data formatting | bytes 4718592 | tf_op jit(solution)/shard_map/reshape | solution.py:67
  103.3 6.1 %copy.83 = bf16[2,9,128,8,64]{2,4,1,3,0:T(8,128)(2,1)} copy(bf16[2,9,128,8,64]{4,3,2,1,0:T(8,128)(2,1)} %reshape.200) | data formatting | bytes 4718592 | tf_op jit(solution)/shard_map/while | solution.py:96
  109.5 2.8 broadcast_in_dim.61
  112.3 76.9 %while.27 = (s32[]{:T(128)}, f32[2,9,128,8,64]{2,4,3,1,0:T(8,128)}, bf16[3,128,8,64]{1,3,2,0:T(8,128)(2,1)S(1)}, s32[3]{0:T(128)S(1)}, s32[3,7]{1,0:T(4,128)S(1)...) while((s32[]{:T(128)}, f32[2,9,128,8,64]{2,4,3,1,0:T(8,128)}, ...), condition=%wide.region_10.11_spmd, body=%wide.region_4.10_spmd.sunk | while | flops 611644544 | bytes 56669256 | solution.py:128
  116.2 2.1 select_reduce_fusion.5
  119.0 2.0 fusion.89
  121.1 2.6 multiply_reduce_fusion.2
  124.9 1.7 fusion.90
  128.9 4.8 %scatter_fusion = f32[2,9,128,8,64]{2,4,3,1,0:T(8,128)} fusion(f32[2,9,128,8,64]{2,4,3,1,0:T(8,128)} %get-tuple-element.398, s32[7]{0:T(128)S(1)} %select_bitcast_fusion.5, f32[7,128,8,64]{1,3,2,0:T(8,128)} %copy.129), kind=kCustom, calls=%fused_computation.clone.1 | custom fusion | flops 458752 | bytes 5505080 | tf_op jit(solution)/shard_map/while/body/eval_jaxpr/scatter-add | solution.py:124
  133.7 4.3 %scatter_fusion.1 = f32[2,9,128,8,64]{2,4,3,1,0:T(8,128)} fusion(f32[2,9,128,8,64]{2,4,3,1,0:T(8,128)} %scatter_fusion, s32[7]{0:T(128)S(1)} %get-tuple-element.349, f32[7,128,8,64]{1,3,2,0:T(8,128)S(1)} %copy.130), kind=kCustom, calls=%fused_computation.1.clone.1 | custom fusion | flops 458752 | bytes 5505080 | tf_op jit(solution)/shard_map/while/body/eval_jaxpr/scatter-add | solution.py:124
  141.9 2.1 select_reduce_fusion.5
  144.7 2.0 fusion.89
  146.8 2.6 multiply_reduce_fusion.2
  150.6 1.7 fusion.90
  154.6 4.8 %scatter_fusion = f32[2,9,128,8,64]{2,4,3,1,0:T(8,128)} fusion(f32[2,9,128,8,64]{2,4,3,1,0:T(8,128)} %get-tuple-element.398, s32[7]{0:T(128)S(1)} %select_bitcast_fusion.5, f32[7,128,8,64]{1,3,2,0:T(8,128)} %copy.129), kind=kCustom, calls=%fused_computation.clone.1 | custom fusion | flops 458752 | bytes 5505080 | tf_op jit(solution)/shard_map/while/body/eval_jaxpr/scatter-add | solution.py:124
  159.4 4.2 %scatter_fusion.1 = f32[2,9,128,8,64]{2,4,3,1,0:T(8,128)} fusion(f32[2,9,128,8,64]{2,4,3,1,0:T(8,128)} %scatter_fusion, s32[7]{0:T(128)S(1)} %get-tuple-element.349, f32[7,128,8,64]{1,3,2,0:T(8,128)S(1)} %copy.130), kind=kCustom, calls=%fused_computation.1.clone.1 | custom fusion | flops 458752 | bytes 5505080 | tf_op jit(solution)/shard_map/while/body/eval_jaxpr/scatter-add | solution.py:124
  167.5 2.1 select_reduce_fusion.5
  170.3 2.0 fusion.89
  172.4 2.6 multiply_reduce_fusion.2
  180.2 4.8 %scatter_fusion = f32[2,9,128,8,64]{2,4,3,1,0:T(8,128)} fusion(f32[2,9,128,8,64]{2,4,3,1,0:T(8,128)} %get-tuple-element.398, s32[7]{0:T(128)S(1)} %select_bitcast_fusion.5, f32[7,128,8,64]{1,3,2,0:T(8,128)} %copy.129), kind=kCustom, calls=%fused_computation.clone.1 | custom fusion | flops 458752 | bytes 5505080 | tf_op jit(solution)/shard_map/while/body/eval_jaxpr/scatter-add | solution.py:124
  185.0 4.2 %scatter_fusion.1 = f32[2,9,128,8,64]{2,4,3,1,0:T(8,128)} fusion(f32[2,9,128,8,64]{2,4,3,1,0:T(8,128)} %scatter_fusion, s32[7]{0:T(128)S(1)} %get-tuple-element.349, f32[7,128,8,64]{1,3,2,0:T(8,128)S(1)} %copy.130), kind=kCustom, calls=%fused_computation.1.clone.1 | custom fusion | flops 458752 | bytes 5505080 | tf_op jit(solution)/shard_map/while/body/eval_jaxpr/scatter-add | solution.py:124
  189.3 2.9 bitcast_convert_fusion
  192.3 5.4 %collective-permute-start.2 = (bf16[2,3,128,512]{2,3,1,0:T(8,128)(2,1)S(1)}, bf16[2,3,128,512]{2,3,1,0:T(8,128)(2,1)}, u32[]{:S(2)}, u32[]{:S(2)}) collective-permute-start(bf16[2,3,128,512]{2,3,1,0:T(8,128)(2,1)S(1)} %get-tuple-element.236), channel_id=1, source_target_pairs={{0,4},{4,8},{8,12},{12,16},{16,20},{20,24},{24,28},{1,5},{5,9},{9,... | collective-permute-start | bytes 2359304 | tf_op jit(solution)/shard_map/ppermute | solution.py:31
  201.6 29.0 %collective-permute-done.2 = bf16[2,3,128,512]{2,3,1,0:T(8,128)(2,1)} collective-permute-done((bf16[2,3,128,512]{2,3,1,0:T(8,128)(2,1)S(1)}, bf16[2,3,128,512]{2,3,1,0:T(8,128)(2,1)}, u32[]{:S(2)}, u32[]{:S(2)}) %collective-permute-start.2) | collective-permute-done | bytes 786464 | tf_op jit(solution)/shard_map/ppermute | solution.py:31
  230.7 2.1 fusion.41
  233.7 4.5 %convolution_convert_fusion = bf16[3,512,1024]{2,1,0:T(8,128)(2,1)} fusion(bf16[384,1,512]{0,2,1:T(8,128)(2,1)S(1)} %copy.97, bf16[384,1,512]{0,2,1:T(8,128)(2,1)S(1)} %copy.96, bf16[384,1,512]{0,2,1:T(8,128)(2,1)} %stack_reshape.3, bf16[1,384,1024]{2,1,0:T(8,128)(2,1)S(1)} %copy-done), kind=kOutput, calls=%fused_computation.64 | convolution fusion | flops 1210712064 | bytes 5111808 | tf_op jit(solution)/shard_map/tr,tcf->rcf/dot_general | solution.py:152
  238.1 4.7 %copy.120 = bf16[1024,1536]{1,0:T(8,128)(2,1)} copy(bf16[1024,1536]{0,1:T(8,128)(2,1)} %bitcast.204) | data formatting | bytes 6291456
  244.2 1.8 fusion.54
  246.0 71.7 %reduce-scatter.4.cloned.1.call-done = bf16[128,1536]{1,0:T(8,128)(2,1)} async-done(((bf16[1024,1536]{1,0:T(8,128)(2,1)}), bf16[128,1536]{1,0:T(8,128)(2,1)}) %reduce-scatter.4.cloned.1.call-update) | async-done | bytes 393232
  320.2 2.0 fusion.60
  324.0 27.1 %while.26 = (s32[]{:T(128)}, bf16[3,128,8,64]{1,3,2,0:T(8,128)(2,1)S(1)}, s32[3]{0:T(128)S(1)}, bf16[2,9,128,8,64]{2,4,1,3,0:T(8,128)(2,1)}, s32[3,7]{1,0:T(4,12...) while((s32[]{:T(128)}, ...), condition=%wide.region_3.4_spmd, body=%wide.region_0.3_spmd.sunk | while | flops 245954576 | bytes 13128970 | solution.py:96
  327.8 2.1 select_reduce_fusion.4
  330.6 2.4 fusion.82
  336.9 2.1 select_reduce_fusion.4
  339.7 2.4 fusion.82
  345.9 2.1 select_reduce_fusion.4
  348.7 2.4 fusion.82
  354.7 15.5 %all-reduce.7.cloned.1.call-done = bf16[1,384,1024]{2,1,0:T(8,128)(2,1)} async-done(((bf16[1,384,1024]{2,1,0:T(8,128)(2,1)}), bf16[1,384,1024]{2,1,0:T(8,128)(2,1)}) %all-reduce.7.cloned.1.call-update) | async-done | bytes 786448 | tf_op jit(solution)/shard_map/psum | solution.py:149
  370.2 2.1 copy.152
  (107 shorter events, 42.3 us)
Async XLA Ops:
  7.2 26.4 %copy-start = (bf16[1,384,1024]{2,1,0:T(8,128)(2,1)S(1)}, bf16[1,384,1024]{2,1,0:T(8,128)(2,1)}, u32[]{:S(2)}) copy-start(bf16[1,384,1024]{2,1,0:T(8,128)(2,1)} %param.18) | copy-start | bytes 2359300
  7.2 26.4 %all-gather.6.cloned.1.call-start = ((), (), s32[]{:S(2)}) async-start(), calls=%async_computation.2 | async-start | bytes 1572864 | tf_op jit(solution)/shard_map/all_gather | solution.py:59
  7.9 48.6 %all-gather.4.cloned.1.call-start = ((), (), s32[]{:S(2)}) async-start(), calls=%async_computation.1 | async-start | bytes 1572864 | tf_op jit(solution)/shard_map/all_gather | solution.py:58
  8.7 57.2 %copy-start.10 = (s32[24,7]{0,1:T(8,128)S(1)}, s32[24,7]{0,1:T(8,128)}, u32[]{:S(2)}) copy-start(s32[24,7]{0,1:T(8,128)} %param.22) | copy-start | bytes 2020
  8.7 57.3 %copy-start.9 = (bf16[1,384,512]{2,1,0:T(8,128)(2,1)S(1)}, bf16[1,384,512]{2,1,0:T(8,128)(2,1)}, u32[]{:S(2)}) copy-start(bf16[1,384,512]{2,1,0:T(8,128)(2,1)} %param.23) | copy-start | bytes 1179652
  8.7 70.7 %all-gather.8.cloned.1.call-start = ((), (), s32[]{:S(2)}) async-start(), calls=%async_computation.3 | async-start | bytes 1572864 | tf_op jit(solution)/shard_map/all_gather | solution.py:57
  9.4 308.3 %reduce-scatter.4.cloned.1.call-start = ((), (), s32[]{:S(2)}) async-start(), calls=%async_computation.5 | async-start | bytes 3538944
  35.4 30.5 %copy-start.4 = (bf16[1,384,512]{2,1,0:T(8,128)(2,1)}, bf16[1,384,512]{2,1,0:T(8,128)(2,1)S(1)}, u32[]{:S(2)}) copy-start(bf16[1,384,512]{2,1,0:T(8,128)(2,1)S(1)} %fusion.44) | copy-start | bytes 1179652
  58.3 0.7 copy-start.5
  59.1 22.9 %collective-permute-start.1 = (bf16[2,384,512]{2,1,0:T(8,128)(2,1)S(1)}, bf16[2,384,512]{2,1,0:T(8,128)(2,1)S(1)}, u32[]{:S(2)}, u32[]{:S(2)}) collective-permute-start(bf16[2,384,512]{2,1,0:T(8,128)(2,1)S(1)} %pad_maximum_fusion.1), channel_id=1, source_target_pairs={{4,0},{8,4},{12,8},{16,12},{20,16},{24,20},{28,24},{5,1},{9,5},{13... | collective-permute-start | bytes 2359304 | tf_op jit(solution)/shard_map/ppermute | solution.py:21
  60.4 36.6 %collective-permute-start = (bf16[2,384,512]{2,1,0:T(8,128)(2,1)S(1)}, bf16[2,384,512]{2,1,0:T(8,128)(2,1)}, u32[]{:S(2)}, u32[]{:S(2)}) collective-permute-start(bf16[2,384,512]{2,1,0:T(8,128)(2,1)S(1)} %pad_maximum_fusion.1), channel_id=1, source_target_pairs={{0,4},{4,8},{8,12},{12,16},{16,20},{20,24},{24,28},{1,5},{5,9},{9,... | collective-permute-start | bytes 2359304 | tf_op jit(solution)/shard_map/ppermute | solution.py:19
  82.1 0.9 copy-start.8
  109.5 2.9 copy-start.11
  189.3 3.1 copy-start.6
  192.3 38.3 %collective-permute-start.2 = (bf16[2,3,128,512]{2,3,1,0:T(8,128)(2,1)S(1)}, bf16[2,3,128,512]{2,3,1,0:T(8,128)(2,1)}, u32[]{:S(2)}, u32[]{:S(2)}) collective-permute-start(bf16[2,3,128,512]{2,3,1,0:T(8,128)(2,1)S(1)} %get-tuple-element.236), channel_id=1, source_target_pairs={{0,4},{4,8},{8,12},{12,16},{16,20},{20,24},{24,28},{1,5},{5,9},{9,... | collective-permute-start | bytes 2359304 | tf_op jit(solution)/shard_map/ppermute | solution.py:31
  197.7 33.0 %collective-permute-start.3 = (bf16[2,3,128,512]{2,3,1,0:T(8,128)(2,1)S(1)}, bf16[2,3,128,512]{2,3,1,0:T(8,128)(2,1)}, u32[]{:S(2)}, u32[]{:S(2)}) collective-permute-start(bf16[2,3,128,512]{2,3,1,0:T(8,128)(2,1)S(1)} %get-tuple-element.237), channel_id=1, source_target_pairs={{4,0},{8,4},{12,8},{16,12},{20,16},{24,20},{28,24},{5,1},{9,5},{13... | collective-permute-start | bytes 2359304 | tf_op jit(solution)/shard_map/ppermute | solution.py:31
  233.0 5.1 %copy-start.1 = (bf16[1,3,128,512]{3,2,1,0:T(8,128)(2,1)}, bf16[1,3,128,512]{3,2,1,0:T(8,128)(2,1)S(1)}, u32[]{:S(2)}) copy-start(bf16[1,3,128,512]{3,2,1,0:T(8,128)(2,1)S(1)} %copy.91) | copy-start | bytes 1179652
  233.2 4.9 %copy-start.2 = (bf16[1,3,128,512]{3,2,1,0:T(8,128)(2,1)}, bf16[1,3,128,512]{3,2,1,0:T(8,128)(2,1)S(1)}, u32[]{:S(2)}) copy-start(bf16[1,3,128,512]{3,2,1,0:T(8,128)(2,1)S(1)} %copy.92) | copy-start | bytes 1179652
  238.1 4.8 %copy-start.12 = (u32[32]{0:T(128)S(1)}, u32[32]{0:T(128)}, u32[]{:S(2)}) copy-start(u32[32]{0:T(128)} %constant.190) | copy-start | bytes 388
  242.9 109.8 %all-reduce.9.cloned.1.call-start = ((), (), s32[]{:S(2)}) async-start(), calls=%async_computation.6 | async-start | bytes 1048576
  246.0 76.2 %copy-start.3 = (bf16[1,3,128,512]{3,2,1,0:T(8,128)(2,1)S(1)}, bf16[1,3,128,512]{3,2,1,0:T(8,128)(2,1)}, u32[]{:S(2)}) copy-start(bf16[1,3,128,512]{3,2,1,0:T(8,128)(2,1)} %copy-done.2) | copy-start | bytes 1179652
  320.2 50.0 %all-reduce.7.cloned.1.call-start = ((), (), s32[]{:S(2)}) async-start(), calls=%async_computation.4 | async-start | bytes 1572864 | tf_op jit(solution)/shard_map/psum | solution.py:149
  320.2 2.1 copy-start.7
Sparse Core Ops, SparseCore 0:
  9.6 23.9 all-gather.5
  35.1 21.2 all-gather.3
  58.0 21.2 all-gather.7
  243.0 74.6 reduce-scatter.3
  320.3 27.6 all-reduce.8
  350.9 19.2 all-reduce.6
where the time goes:
time: 381 us; the launch traced here: 379 us
  waiting for transfers between devices  189 us (50%)
  matrix products  56 us (15%)
  other arithmetic  43.8 us (11%)
  local copies, waits for them, and re-layouts  41.8 us (11%)
  loops' own time  19.7 us (5%)
  between operations  15.1 us (4%)
  starting transfers between devices  13.9 us (4%)
    unnamed x8, waiting for transfers between devices  73.8 us
    ppermute x2, waiting for transfers between devices, shifted(): lax.ppermute(value, axis, [(source, source + steps) for source in range(l...  29 us
    scatter-add x6, other arithmetic, backward(): running.at[0, slot_rows].add(key_part).at[1, slot_rows].add(value_part)  27.2 us
    all_gather x1, waiting for transfers between devices, per_device(): lax.all_gather(w_value, 'dp', axis=0, tiled=True)  24.1 us
    all_gather x1, waiting for transfers between devices, per_device(): lax.all_gather(w_key, 'dp', axis=0, tiled=True)  21.1 us
    psum x1, waiting for transfers between devices, per_device(): grad_input = lax.psum(partial_input.astype(jnp.bfloat16), 'section')[None]  15.5 us
    ppermute x1, waiting for transfers between devices, extended(): lax.ppermute(tail, axis, [(i, (i + 1) % count) for i in range(ends)])  14.1 us
    unnamed x34, local copies, waits for them, and re-layouts  12.8 us
  transfers between devices with their start and end apart: 10, of which 7 were waited for; matrix products, arithmetic and copies ran while one was open for 10% of the time, Pallas kernels for 0%

commit v1 on v0

--- a/solution.py
+++ b/solution.py
@@ -1,3 +1,4 @@
+import functools
 import jax
 import jax.numpy as jnp
 from jax import lax
@@ -6,6 +7,25 @@
 HD = 64
 BLOCK = 128
 REACH = 3
+
+
+def get_floor(in_array, shard_axis):
+    v_now, frame_out, passed = (
+        lax.axis_size(shard_axis),
+        lax.axis_index(shard_axis),
+        in_array.shape[0],
+    )
+    z, arr_now = (in_array, 1)
+    while arr_now < v_now:
+        stack_in = []
+        for b in [*range(v_now)]:
+            stack_in.append((b, (b - arr_now) % v_now))
+        z = jnp.concatenate([z, lax.ppermute(z, shard_axis, stack_in)], 0)
+        arr_now = 2 * arr_now
+    return jnp.roll(z, frame_out * passed, 0)
+
+
+point_modes = functools.partial(get_floor, shard_axis="dp")
 
 
 def extended(cells, sides, width):
@@ -56,7 +76,7 @@
     query_full, key_full, value_full = (
         lax.all_gather(w_query, "dp", axis=0, tiled=True),
         lax.all_gather(w_key, "dp", axis=0, tiled=True),
-        lax.all_gather(w_value, "dp", axis=0, tiled=True),
+        point_modes(w_value),
     )
     queries = jnp.dot(tokens, query_full, preferred_element_type=jnp.float32).astype(jnp.bfloat16)
     key_rows = jnp.dot(tokens, key_full, preferred_element_type=jnp.float32).astype(jnp.bfloat16)

time: 381 us -> 361 us (0.948)
  waiting for transfers between devices: 189 us -> 160 us
    all_gather x1 -> x0, waiting for transfers between devices: 24.1 us -> none  [per_device(): lax.all_gather(w_value, 'dp', axis=0, tiled=True)]
    all_gather x1, waiting for transfers between devices: 21.1 us -> 3.79 us  [per_device(): lax.all_gather(w_key, 'dp', axis=0, tiled=True)]
    ppermute x0 -> x1, waiting for transfers between devices: none -> 14.8 us  [get_floor(): z = jnp.concatenate([z, lax.ppermute(z, shard_axis, stack_in)], 0)]
    unnamed x34 -> x36, local copies, waits for them, and re-layouts: 12.8 us -> 13.8 us
    unnamed x8 -> x7, waiting for transfers between devices: 73.8 us -> 73.4 us
  transfers between devices with their start and end apart: 10 -> 10, of which waited for: 7 -> 7; matrix products, arithmetic and copies ran while one was open for 10% -> 12% of each run, Pallas kernels for 0% -> 0%
where the time goes in v1:
time: 361 us; the launch traced here: 359 us
  waiting for transfers between devices  160 us (44%)
  matrix products  55.5 us (15%)
  other arithmetic  47.3 us (13%)
  local copies, waits for them, and re-layouts  45.6 us (13%)
  loops' own time  19.7 us (5%)
  starting transfers between devices  16.6 us (5%)
  between operations  14.8 us (4%)
    unnamed x7, waiting for transfers between devices  73.4 us
    ppermute x2, waiting for transfers between devices, shifted(): lax.ppermute(value, axis, [(source, source + steps) for source in range(l...  29.2 us
    scatter-add x6, other arithmetic, backward(): running.at[0, slot_rows].add(key_part).at[1, slot_rows].add(value_part)  27.3 us
    psum x1, waiting for transfers between devices, per_device(): grad_input = lax.psum(partial_input.astype(jnp.bfloat16), 'section')[None]  15.5 us
    ppermute x1, waiting for transfers between devices, get_floor(): z = jnp.concatenate([z, lax.ppermute(z, shard_axis, stack_in)], 0)  14.8 us
    unnamed x36, local copies, waits for them, and re-layouts  13.8 us
    dot_general x6, matrix products, attend(): jnp.einsum('qhd,skhd->hqsk', query_block, key_window, preferred_element_t...  12.4 us
    all_gather x1, waiting for transfers between devices, per_device(): lax.all_gather(w_query, 'dp', axis=0, tiled=True)  11.5 us
  transfers between devices with their start and end apart: 10, of which 7 were waited for; matrix products, arithmetic and copies ran while one was open for 12% of the time, Pallas kernels for 0%

profile of v1, /device:TPU:0, one launch (start us, length us, event | category | flops | bytes accessed | tf_op | source)
XLA Modules:
  0.0 359.0 jit_solution(8128511277250987157)
XLA Ops:
  8.0 3.0 collective-permute-start
  11.1 14.8 %collective-permute-done = bf16[512,512]{1,0:T(8,128)(2,1)S(1)} collective-permute-done((bf16[512,512]{1,0:T(8,128)(2,1)}, bf16[512,512]{1,0:T(8,128)(2,1)S(1)}, u32[]{:S(2)}, u32[]{:S(2)}) %collective-permute-start) | collective-permute-done | bytes 524320 | tf_op jit(solution)/shard_map/ppermute | solution.py:23
  25.9 3.4 fusion.52
  30.8 3.8 %all-gather.3.cloned.1.call-done = bf16[1024,512]{1,0:T(8,128)(2,1)} async-done(((bf16[512,512]{1,0:T(8,128)(2,1)}), bf16[1024,512]{1,0:T(8,128)(2,1)}) %all-gather.3.cloned.1.call-update) | async-done | bytes 1048592 | tf_op jit(solution)/shard_map/all_gather | solution.py:78
  34.6 1.8 fusion.43
  38.5 5.5 %collective-permute-start.1 = (bf16[2,384,512]{2,1,0:T(8,128)(2,1)S(1)}, bf16[2,384,512]{2,1,0:T(8,128)(2,1)}, u32[]{:S(2)}, u32[]{:S(2)}) collective-permute-start(bf16[2,384,512]{2,1,0:T(8,128)(2,1)S(1)} %pad_maximum_fusion.1), channel_id=1, source_target_pairs={{0,4},{4,8},{8,12},{12,16},{16,20},{20,24},{24,28},{1,5},{5,9},{9,... | collective-permute-start | bytes 2359304 | tf_op jit(solution)/shard_map/ppermute | solution.py:39
  47.5 11.5 %all-gather.5.cloned.1.call-done = bf16[1024,512]{1,0:T(8,128)(2,1)} async-done(((bf16[512,512]{1,0:T(8,128)(2,1)}), bf16[1024,512]{1,0:T(8,128)(2,1)}) %all-gather.5.cloned.1.call-update) | async-done | bytes 1048592 | tf_op jit(solution)/shard_map/all_gather | solution.py:77
  59.0 2.5 convolution_convert_fusion.2
  64.4 11.2 %collective-permute-done.1 = bf16[2,384,512]{2,1,0:T(8,128)(2,1)} collective-permute-done((bf16[2,384,512]{2,1,0:T(8,128)(2,1)S(1)}, bf16[2,384,512]{2,1,0:T(8,128)(2,1)}, u32[]{:S(2)}, u32[]{:S(2)}) %collective-permute-start.1) | collective-permute-done | bytes 786464 | tf_op jit(solution)/shard_map/ppermute | solution.py:39
  75.6 1.8 pad_maximum_fusion
  77.4 4.4 %reshape.200 = bf16[2,9,128,8,64]{4,3,2,1,0:T(8,128)(2,1)} reshape(bf16[2,1152,512]{2,1,0:T(8,128)(2,1)S(1)} %pad_maximum_fusion) | data formatting | bytes 4718592 | tf_op jit(solution)/shard_map/reshape | solution.py:87
  81.8 6.1 %copy.83 = bf16[2,9,128,8,64]{2,4,1,3,0:T(8,128)(2,1)} copy(bf16[2,9,128,8,64]{4,3,2,1,0:T(8,128)(2,1)} %reshape.200) | data formatting | bytes 4718592 | tf_op jit(solution)/shard_map/while | solution.py:116
  88.0 2.8 broadcast_in_dim.61
  90.8 77.0 %while.27 = (s32[]{:T(128)}, f32[2,9,128,8,64]{2,4,3,1,0:T(8,128)}, bf16[3,128,8,64]{1,3,2,0:T(8,128)(2,1)S(1)}, s32[3]{0:T(128)S(1)}, s32[3,7]{1,0:T(4,128)S(1)...) while((s32[]{:T(128)}, f32[2,9,128,8,64]{2,4,3,1,0:T(8,128)}, ...), condition=%wide.region_10.11_spmd, body=%wide.region_4.10_spmd.sunk | while | flops 611644544 | bytes 56669256 | solution.py:148
  94.7 2.1 select_reduce_fusion.5
  97.5 2.0 fusion.92
  99.6 2.6 multiply_reduce_fusion.2
  107.4 4.8 %scatter_fusion = f32[2,9,128,8,64]{2,4,3,1,0:T(8,128)} fusion(f32[2,9,128,8,64]{2,4,3,1,0:T(8,128)} %get-tuple-element.398, s32[7]{0:T(128)S(1)} %select_bitcast_fusion.5, f32[7,128,8,64]{1,3,2,0:T(8,128)} %copy.129), kind=kCustom, calls=%fused_computation.clone.1 | custom fusion | flops 458752 | bytes 5505080 | tf_op jit(solution)/shard_map/while/body/eval_jaxpr/scatter-add | solution.py:144
  112.2 4.3 %scatter_fusion.1 = f32[2,9,128,8,64]{2,4,3,1,0:T(8,128)} fusion(f32[2,9,128,8,64]{2,4,3,1,0:T(8,128)} %scatter_fusion, s32[7]{0:T(128)S(1)} %get-tuple-element.349, f32[7,128,8,64]{1,3,2,0:T(8,128)S(1)} %copy.130), kind=kCustom, calls=%fused_computation.1.clone.1 | custom fusion | flops 458752 | bytes 5505080 | tf_op jit(solution)/shard_map/while/body/eval_jaxpr/scatter-add | solution.py:144
  120.3 2.1 select_reduce_fusion.5
  123.1 2.0 fusion.92
  125.3 2.6 multiply_reduce_fusion.2
  129.0 1.7 fusion.93
  133.1 4.8 %scatter_fusion = f32[2,9,128,8,64]{2,4,3,1,0:T(8,128)} fusion(f32[2,9,128,8,64]{2,4,3,1,0:T(8,128)} %get-tuple-element.398, s32[7]{0:T(128)S(1)} %select_bitcast_fusion.5, f32[7,128,8,64]{1,3,2,0:T(8,128)} %copy.129), kind=kCustom, calls=%fused_computation.clone.1 | custom fusion | flops 458752 | bytes 5505080 | tf_op jit(solution)/shard_map/while/body/eval_jaxpr/scatter-add | solution.py:144
  137.9 4.3 %scatter_fusion.1 = f32[2,9,128,8,64]{2,4,3,1,0:T(8,128)} fusion(f32[2,9,128,8,64]{2,4,3,1,0:T(8,128)} %scatter_fusion, s32[7]{0:T(128)S(1)} %get-tuple-element.349, f32[7,128,8,64]{1,3,2,0:T(8,128)S(1)} %copy.130), kind=kCustom, calls=%fused_computation.1.clone.1 | custom fusion | flops 458752 | bytes 5505080 | tf_op jit(solution)/shard_map/while/body/eval_jaxpr/scatter-add | solution.py:144
  146.0 2.1 select_reduce_fusion.5
  148.8 2.0 fusion.92
  150.9 2.6 multiply_reduce_fusion.2
  158.7 4.8 %scatter_fusion = f32[2,9,128,8,64]{2,4,3,1,0:T(8,128)} fusion(f32[2,9,128,8,64]{2,4,3,1,0:T(8,128)} %get-tuple-element.398, s32[7]{0:T(128)S(1)} %select_bitcast_fusion.5, f32[7,128,8,64]{1,3,2,0:T(8,128)} %copy.129), kind=kCustom, calls=%fused_computation.clone.1 | custom fusion | flops 458752 | bytes 5505080 | tf_op jit(solution)/shard_map/while/body/eval_jaxpr/scatter-add | solution.py:144
  163.5 4.2 %scatter_fusion.1 = f32[2,9,128,8,64]{2,4,3,1,0:T(8,128)} fusion(f32[2,9,128,8,64]{2,4,3,1,0:T(8,128)} %scatter_fusion, s32[7]{0:T(128)S(1)} %get-tuple-element.349, f32[7,128,8,64]{1,3,2,0:T(8,128)S(1)} %copy.130), kind=kCustom, calls=%fused_computation.1.clone.1 | custom fusion | flops 458752 | bytes 5505080 | tf_op jit(solution)/shard_map/while/body/eval_jaxpr/scatter-add | solution.py:144
  167.8 2.9 bitcast_convert_fusion
  170.8 5.4 %collective-permute-start.3 = (bf16[2,3,128,512]{2,3,1,0:T(8,128)(2,1)S(1)}, bf16[2,3,128,512]{2,3,1,0:T(8,128)(2,1)}, u32[]{:S(2)}, u32[]{:S(2)}) collective-permute-start(bf16[2,3,128,512]{2,3,1,0:T(8,128)(2,1)S(1)} %get-tuple-element.236), channel_id=1, source_target_pairs={{0,4},{4,8},{8,12},{12,16},{16,20},{20,24},{24,28},{1,5},{5,9},{9,... | collective-permute-start | bytes 2359304 | tf_op jit(solution)/shard_map/ppermute | solution.py:51
  179.9 29.2 %collective-permute-done.3 = bf16[2,3,128,512]{2,3,1,0:T(8,128)(2,1)} collective-permute-done((bf16[2,3,128,512]{2,3,1,0:T(8,128)(2,1)S(1)}, bf16[2,3,128,512]{2,3,1,0:T(8,128)(2,1)}, u32[]{:S(2)}, u32[]{:S(2)}) %collective-permute-start.3) | collective-permute-done | bytes 786464 | tf_op jit(solution)/shard_map/ppermute | solution.py:51
  209.2 2.2 fusion.41
  212.9 4.4 %convolution_convert_fusion = bf16[3,512,1024]{2,1,0:T(8,128)(2,1)} fusion(bf16[384,1,512]{0,2,1:T(8,128)(2,1)S(1)} %copy.97, bf16[384,1,512]{0,2,1:T(8,128)(2,1)} %copy.96, bf16[384,1,512]{0,2,1:T(8,128)(2,1)S(1)} %copy-done.10, bf16[1,384,1024]{2,1,0:T(8,128)(2,1)S(1)} %copy-done), kind=kOutput, calls=%fused_computation.64 | convolution fusion | flops 1210712064 | bytes 5111808 | tf_op jit(solution)/shard_map/tr,tcf->rcf/dot_general | solution.py:172
  217.4 4.7 %copy.120 = bf16[1024,1536]{1,0:T(8,128)(2,1)} copy(bf16[1024,1536]{0,1:T(8,128)(2,1)} %bitcast.206) | data formatting | bytes 6291456
  223.5 1.8 fusion.57
  225.3 72.7 %reduce-scatter.4.cloned.1.call-done = bf16[128,1536]{1,0:T(8,128)(2,1)} async-done(((bf16[1024,1536]{1,0:T(8,128)(2,1)}), bf16[128,1536]{1,0:T(8,128)(2,1)}) %reduce-scatter.4.cloned.1.call-update) | async-done | bytes 393232
  300.5 2.0 fusion.63
  304.3 27.1 %while.26 = (s32[]{:T(128)}, bf16[3,128,8,64]{1,3,2,0:T(8,128)(2,1)S(1)}, s32[3]{0:T(128)S(1)}, bf16[2,9,128,8,64]{2,4,1,3,0:T(8,128)(2,1)}, s32[3,7]{1,0:T(4,12...) while((s32[]{:T(128)}, ...), condition=%wide.region_3.4_spmd, body=%wide.region_0.3_spmd.sunk | while | flops 245954576 | bytes 13128970 | solution.py:116
  308.1 2.1 select_reduce_fusion.4
  310.9 2.4 fusion.85
  317.1 2.1 select_reduce_fusion.4
  319.9 2.4 fusion.85
  326.2 2.1 select_reduce_fusion.4
  329.0 2.4 fusion.85
  334.9 15.5 %all-reduce.7.cloned.1.call-done = bf16[1,384,1024]{2,1,0:T(8,128)(2,1)} async-done(((bf16[1,384,1024]{2,1,0:T(8,128)(2,1)}), bf16[1,384,1024]{2,1,0:T(8,128)(2,1)}) %all-reduce.7.cloned.1.call-update) | async-done | bytes 786448 | tf_op jit(solution)/shard_map/psum | solution.py:169
  350.5 2.1 copy.152
  (109 shorter events, 46.9 us)
Async XLA Ops:
  7.2 23.0 %copy-start = (bf16[1,384,1024]{2,1,0:T(8,128)(2,1)S(1)}, bf16[1,384,1024]{2,1,0:T(8,128)(2,1)}, u32[]{:S(2)}) copy-start(bf16[1,384,1024]{2,1,0:T(8,128)(2,1)} %param.18) | copy-start | bytes 2359300
  7.2 27.4 %all-gather.3.cloned.1.call-start = ((), (), s32[]{:S(2)}) async-start(), calls=%async_computation.1 | async-start | bytes 1572864 | tf_op jit(solution)/shard_map/all_gather | solution.py:78
  7.9 51.0 %all-gather.5.cloned.1.call-start = ((), (), s32[]{:S(2)}) async-start(), calls=%async_computation.2 | async-start | bytes 1572864 | tf_op jit(solution)/shard_map/all_gather | solution.py:77
  8.0 17.9 %collective-permute-start = (bf16[512,512]{1,0:T(8,128)(2,1)}, bf16[512,512]{1,0:T(8,128)(2,1)S(1)}, u32[]{:S(2)}, u32[]{:S(2)}) collective-permute-start(bf16[512,512]{1,0:T(8,128)(2,1)} %param.21), channel_id=1, source_target_pairs={{0,2},{2,0},{1,3},{3,1},{4,6},{6,4},{5,7},{7,5},{8,10},{10,8},{9,1... | collective-permute-start | bytes 1572872 | tf_op jit(solution)/shard_map/ppermute | solution.py:23
  11.0 287.0 %reduce-scatter.4.cloned.1.call-start = ((), (), s32[]{:S(2)}) async-start(), calls=%async_computation.4 | async-start | bytes 3538944
  29.2 1.0 copy-start.1
  30.2 13.8 %copy-start.11 = (s32[24,7]{0,1:T(8,128)S(1)}, s32[24,7]{0,1:T(8,128)}, u32[]{:S(2)}) copy-start(s32[24,7]{0,1:T(8,128)} %param.22) | copy-start | bytes 2020
  30.8 30.7 %copy-start.6 = (bf16[1,384,512]{2,1,0:T(8,128)(2,1)}, bf16[1,384,512]{2,1,0:T(8,128)(2,1)S(1)}, u32[]{:S(2)}) copy-start(bf16[1,384,512]{2,1,0:T(8,128)(2,1)S(1)} %fusion.44) | copy-start | bytes 1179652
  36.4 0.7 copy-start.7
  37.2 26.3 %collective-permute-start.2 = (bf16[2,384,512]{2,1,0:T(8,128)(2,1)S(1)}, bf16[2,384,512]{2,1,0:T(8,128)(2,1)S(1)}, u32[]{:S(2)}, u32[]{:S(2)}) collective-permute-start(bf16[2,384,512]{2,1,0:T(8,128)(2,1)S(1)} %pad_maximum_fusion.1), channel_id=1, source_target_pairs={{4,0},{8,4},{12,8},{16,12},{20,16},{24,20},{28,24},{5,1},{9,5},{13... | collective-permute-start | bytes 2359304 | tf_op jit(solution)/shard_map/ppermute | solution.py:41
  38.5 37.1 %collective-permute-start.1 = (bf16[2,384,512]{2,1,0:T(8,128)(2,1)S(1)}, bf16[2,384,512]{2,1,0:T(8,128)(2,1)}, u32[]{:S(2)}, u32[]{:S(2)}) collective-permute-start(bf16[2,384,512]{2,1,0:T(8,128)(2,1)S(1)} %pad_maximum_fusion.1), channel_id=1, source_target_pairs={{0,4},{4,8},{8,12},{12,16},{16,20},{20,24},{24,28},{1,5},{5,9},{9,... | collective-permute-start | bytes 2359304 | tf_op jit(solution)/shard_map/ppermute | solution.py:39
  63.5 0.9 copy-start.9
  87.9 2.9 copy-start.12
  167.8 3.1 copy-start.8
  170.8 38.3 %collective-permute-start.3 = (bf16[2,3,128,512]{2,3,1,0:T(8,128)(2,1)S(1)}, bf16[2,3,128,512]{2,3,1,0:T(8,128)(2,1)}, u32[]{:S(2)}, u32[]{:S(2)}) collective-permute-start(bf16[2,3,128,512]{2,3,1,0:T(8,128)(2,1)S(1)} %get-tuple-element.236), channel_id=1, source_target_pairs={{0,4},{4,8},{8,12},{12,16},{16,20},{20,24},{24,28},{1,5},{5,9},{9,... | collective-permute-start | bytes 2359304 | tf_op jit(solution)/shard_map/ppermute | solution.py:51
  176.2 32.9 %collective-permute-start.4 = (bf16[2,3,128,512]{2,3,1,0:T(8,128)(2,1)S(1)}, bf16[2,3,128,512]{2,3,1,0:T(8,128)(2,1)}, u32[]{:S(2)}, u32[]{:S(2)}) collective-permute-start(bf16[2,3,128,512]{2,3,1,0:T(8,128)(2,1)S(1)} %get-tuple-element.237), channel_id=1, source_target_pairs={{4,0},{8,4},{12,8},{16,12},{20,16},{24,20},{28,24},{5,1},{9,5},{13... | collective-permute-start | bytes 2359304 | tf_op jit(solution)/shard_map/ppermute | solution.py:51
  209.2 3.8 %copy-start.10 = (bf16[384,1,512]{0,2,1:T(8,128)(2,1)S(1)}, bf16[384,1,512]{0,2,1:T(8,128)(2,1)}, u32[]{:S(2)}) copy-start(bf16[384,1,512]{0,2,1:T(8,128)(2,1)} %stack_reshape.3) | copy-start | bytes 1179652
  211.6 5.8 %copy-start.3 = (bf16[1,3,128,512]{3,2,1,0:T(8,128)(2,1)}, bf16[1,3,128,512]{3,2,1,0:T(8,128)(2,1)S(1)}, u32[]{:S(2)}) copy-start(bf16[1,3,128,512]{3,2,1,0:T(8,128)(2,1)S(1)} %copy.91) | copy-start | bytes 1179652
  211.8 5.6 %copy-start.4 = (bf16[1,3,128,512]{3,2,1,0:T(8,128)(2,1)}, bf16[1,3,128,512]{3,2,1,0:T(8,128)(2,1)S(1)}, u32[]{:S(2)}) copy-start(bf16[1,3,128,512]{3,2,1,0:T(8,128)(2,1)S(1)} %copy.92) | copy-start | bytes 1179652
  217.4 4.8 %copy-start.13 = (u32[32]{0:T(128)S(1)}, u32[32]{0:T(128)}, u32[]{:S(2)}) copy-start(u32[32]{0:T(128)} %constant.217) | copy-start | bytes 388
  222.1 110.9 %all-reduce.9.cloned.1.call-start = ((), (), s32[]{:S(2)}) async-start(), calls=%async_computation.5 | async-start | bytes 1048576
  225.3 77.3 %copy-start.5 = (bf16[1,3,128,512]{3,2,1,0:T(8,128)(2,1)S(1)}, bf16[1,3,128,512]{3,2,1,0:T(8,128)(2,1)}, u32[]{:S(2)}) copy-start(bf16[1,3,128,512]{3,2,1,0:T(8,128)(2,1)} %copy-done.4) | copy-start | bytes 1179652
  300.5 50.0 %all-reduce.7.cloned.1.call-start = ((), (), s32[]{:S(2)}) async-start(), calls=%async_computation.3 | async-start | bytes 1572864 | tf_op jit(solution)/shard_map/psum | solution.py:169
  300.5 2.1 copy-start.2
Sparse Core Ops, SparseCore 0:
  9.6 24.9 all-gather.2
  36.1 22.7 all-gather.4
  222.3 75.6 reduce-scatter.3
  300.6 27.6 all-reduce.8
  331.2 19.2 all-reduce.6
